TPU v7x, 128 devices: a whole 4x4x4 slice. The times are simulated.
128 devices in a mesh: row: 8 (over z, core), col: 16 (over y, x).
Axes of the slice: x: 4, y: 4, z: 4, core: 2. Of those that a mesh axis runs over, the one named last changes fastest.
Arguments:
- psi_val: float32 [64, 128, 128, 128], P(None, 'row', 'col'), may hold values from -6 to 6
- psi_cond: float32 [64, 128, 128, 128], P(None, 'row', 'col'), may hold values from -6 to 6
- eps_val: float32 [64], replicated, may hold values from -12 to -1
- eps_cond: float32 [64], replicated, may hold values from 1 to 12
- val_index: int32 [128], replicated, may hold values from 0 to 63
- cond_index: int32 [128], replicated, may hold values from 0 to 63
- gmap: int32 [8192], replicated, may hold values from 0 to 2097151, as said below
- chi0_in: float32 [2, 8192, 8192], P(None, 'row', 'col'), may hold values from -6 to 6
Outputs:
- chi0_out: float32 [2, 8192, 8192], P(None, 'row', 'col')
Inputs may be any that keep to these rules, and one draw needn't show every extreme that they name: gmap holds 8192 distinct entries. Entries g of device block d = g // 64 (d = r * 16 + c) have ky in [r * 16, (r + 1) * 16) and kz in [c * 8, (c + 1) * 8); kx is any.
All inputs are finite; a program needn't handle non-finite values.
Results may differ from a plain program's by a relative error of at most 0.000068.
Values sent between devices are 32-bit elements; how exact they have to be, the bound alone decides.
No kernel may reach another device: no remote copies, remote signals or barrier semaphores. Data moves between devices by JAX's collectives and lax.ppermute only.
A program may use at most 128 MiB of HBM per device.

v0:
```python
import math
import jax
import jax.numpy as jnp
from jax import lax
from jax.sharding import PartitionSpec as P

GRID = 128
NG = 8192
HIGH = lax.Precision.HIGHEST


def spread(block, axis, holder):
    block = jnp.where(lax.axis_index(axis) == holder, block, jnp.zeros_like(block))
    return lax.psum(block, axis)


def dft_tables(length):
    steps = jnp.arange(length, dtype=jnp.int32)
    phase = steps[:, None] * steps[None, :] % length
    angle = phase.astype(jnp.float32) * (2.0 * math.pi / length)
    return (jnp.cos(angle), jnp.sin(angle))


def point_tables(freq_x, length):
    steps = jnp.arange(length, dtype=jnp.int32)
    phase = steps[:, None] * freq_x[None, :] % length
    angle = phase.astype(jnp.float32) * (2.0 * math.pi / length)
    return (jnp.cos(angle), jnp.sin(angle))


def pick_points(real_part, imag_part, yz_index, cos_x, sin_x):
    count = real_part.shape[0]
    flat_re = real_part.reshape(count, real_part.shape[1], -1)
    flat_im = imag_part.reshape(count, imag_part.shape[1], -1)
    cols_re = jnp.take(flat_re, yz_index, axis=2)
    cols_im = jnp.take(flat_im, yz_index, axis=2)
    m_re = jnp.sum(cols_re * cos_x[None] + cols_im * sin_x[None], axis=1)
    m_im = jnp.sum(cols_im * cos_x[None] - cols_re * sin_x[None], axis=1)
    return (m_re, m_im)


def contract_pairs(left, right):
    return lax.dot_general(
        left, right, (((0,), (0,)), ((), ())), precision=HIGH, preferred_element_type=jnp.float32
    )


def on_device(psi_val, psi_cond, eps_val, eps_cond, val_index, cond_index, gmap, chi0_in):
    pairs = val_index.shape[0]
    scale = 1.0 / math.sqrt(GRID**3)
    cos_t, sin_t = dft_tables(GRID)
    rho = jnp.take(psi_val, val_index, axis=0) * jnp.take(psi_cond, cond_index, axis=0)
    row_pos = lax.axis_index("row")
    col_pos = lax.axis_index("col")
    mesh_cols = lax.axis_size("col")
    mesh_rows = lax.axis_size("row")
    per_device = NG // (mesh_rows * mesh_cols)
    row_span = GRID // mesh_rows
    col_span = GRID // mesh_cols
    flat_pos = row_pos * mesh_cols + col_pos
    own_map = lax.dynamic_slice_in_dim(gmap, flat_pos * per_device, per_device, 0)
    freq_x = own_map // (GRID * GRID)
    freq_y = own_map // GRID % GRID - row_pos * row_span
    freq_z = own_map % GRID - col_pos * col_span
    yz_index = freq_y * col_span + freq_z
    cos_x, sin_x = point_tables(freq_x, GRID)
    z_re = jnp.einsum("pxyz,zk->pxyk", rho, cos_t, precision=HIGH)
    z_im = -jnp.einsum("pxyz,zk->pxyk", rho, sin_t, precision=HIGH)
    part_re = lax.all_to_all(z_re, "col", split_axis=3, concat_axis=2, tiled=True)
    part_im = lax.all_to_all(z_im, "col", split_axis=3, concat_axis=2, tiled=True)
    y_re = jnp.einsum("pxyz,yk->pxkz", part_re, cos_t, precision=HIGH) + jnp.einsum(
        "pxyz,yk->pxkz", part_im, sin_t, precision=HIGH
    )
    y_im = jnp.einsum("pxyz,yk->pxkz", part_im, cos_t, precision=HIGH) - jnp.einsum(
        "pxyz,yk->pxkz", part_re, sin_t, precision=HIGH
    )
    y_re, y_im = (y_re, y_im)
    m_re, m_im = pick_points(
        lax.all_to_all(y_re, "row", split_axis=2, concat_axis=1, tiled=True),
        lax.all_to_all(y_im, "row", split_axis=2, concat_axis=1, tiled=True),
        yz_index,
        cos_x,
        sin_x,
    )
    m_re = m_re * scale
    m_im = m_im * scale
    cols_span = chi0_in.shape[2]
    rows_re, rows_im = (
        lax.all_gather(m_re, "col", axis=1, tiled=True),
        lax.all_gather(m_im, "col", axis=1, tiled=True),
    )
    offset = col_pos * mesh_rows % mesh_cols * per_device
    piece_re = lax.dynamic_slice_in_dim(rows_re, offset, cols_span, 1)
    piece_im = lax.dynamic_slice_in_dim(rows_im, offset, cols_span, 1)
    root = col_pos * mesh_rows // mesh_cols
    cols_re, cols_im = (spread(piece_re, "row", root), spread(piece_im, "row", root))
    val_hot = val_index[:, None] == jnp.arange(eps_val.shape[0], dtype=jnp.int32)[None, :]
    cond_hot = cond_index[:, None] == jnp.arange(eps_cond.shape[0], dtype=jnp.int32)[None, :]
    energy_v = jnp.sum(jnp.where(val_hot, eps_val[None, :], 0.0), axis=1)
    energy_c = jnp.sum(jnp.where(cond_hot, eps_cond[None, :], 0.0), axis=1)
    weight = (-6.0 / (math.sqrt(pairs) * (energy_c - energy_v)))[:, None]
    out_re = (
        chi0_in[0]
        + contract_pairs(weight * rows_re, cols_re)
        + contract_pairs(weight * rows_im, cols_im)
    )
    out_im = (
        chi0_in[1]
        + contract_pairs(weight * rows_im, cols_re)
        - contract_pairs(weight * rows_re, cols_im)
    )
    return jnp.stack([out_re, out_im])


def solution(mesh):
    return jax.shard_map(
        on_device,
        mesh=mesh,
        in_specs=(
            P(None, "row", "col", None),
            P(None, "row", "col", None),
            P(),
            P(),
            P(),
            P(),
            P(),
            P(None, "row", "col"),
        ),
        out_specs=P(None, "row", "col"),
        check_vma=False,
    )
```

profile of v0, /device:TPU:0, one launch (start us, length us, event | category | flops | bytes accessed | tf_op | source)
XLA Modules:
  0.0 716.1 jit_solution(10853611819511883215)
XLA Ops:
  7.9 6.5 gather_fusion.1
  14.4 6.5 gather_fusion
  20.9 6.5 select_multiply_fusion
  30.7 14.7 %fusion.6 = f32[128,16,8,128]{3,0,2,1:T(8,128)} fusion(f32[128,16,8,128]{3,2,1,0:T(8,128)S(1)} %select_multiply_fusion), kind=kOutput, calls=%fused_computation.18 | convolution fusion | flops 3223552000 | bytes 16777216 | tf_op jit(solution)/shard_map/pxyz,zk->pxyk/dot_general | solution.py:68
  45.4 9.3 %copy.79 = f32[128,16,8,128]{0,2,1,3:T(8,128)} copy(f32[128,16,8,128]{3,0,2,1:T(8,128)} %fusion.6) | data formatting | bytes 16777216 | tf_op jit(solution)/shard_map/neg | solution.py:68
  54.7 7.4 %all-to-all-start.1 = ((f32[128,16,8,128]{0,2,1,3:T(8,128)}), f32[128,16,8,128]{0,2,1,3:T(8,128)}, u32[]{:S(2)}, u32[]{:S(2)}) async-start(f32[128,16,8,128]{0,2,1,3:T(8,128)} %copy.79), calls=%async_computation.1 | async-start | bytes 16777216 | tf_op jit(solution)/shard_map/all_to_all | solution.py:70
  62.1 11.3 %fusion.29 = f32[128,16,8,128]{3,2,1,0:T(8,128)} fusion(f32[128,16,8,128]{3,2,1,0:T(8,128)} %copy-done), kind=kOutput, calls=%fused_computation.46 | convolution fusion | flops 3221454848 | bytes 16777216 | tf_op jit(solution)/shard_map/pxyz,zk->pxyk/dot_general | solution.py:67
  73.4 9.3 %copy.73 = f32[128,16,8,128]{0,2,1,3:T(8,128)} copy(f32[128,16,8,128]{3,2,1,0:T(8,128)} %fusion.29) | data formatting | bytes 16777216 | tf_op jit(solution)/shard_map/pxyz,zk->pxyk/dot_general | solution.py:67
  82.7 103.4 %all-to-all-done.1 = f32[128,16,8,128]{0,2,1,3:T(8,128)} async-done(((f32[128,16,8,128]{0,2,1,3:T(8,128)}), f32[128,16,8,128]{0,2,1,3:T(8,128)}, u32[]{:S(2)}, u32[]{:S(2)}) %all-to-all-start.1) | async-done | bytes 8388640 | tf_op jit(solution)/shard_map/all_to_all | solution.py:70
  186.1 5.7 all-to-all-start
  191.9 11.5 %copy.81 = f32[128,16,16,8,8]{0,4,3,2,1:T(8,128)} copy(f32[128,16,16,8,8]{0,3,1,4,2:T(8,128)} %bitcast.13) | data formatting | bytes 16777216 | tf_op jit(solution)/shard_map/all_to_all | solution.py:70
  203.3 9.3 %copy.82 = f32[128,16,128,8]{2,0,3,1:T(8,128)} copy(f32[128,16,128,8]{0,3,2,1:T(8,128)} %bitcast.83) | data formatting | bytes 16777216 | tf_op jit(solution)/shard_map/all_to_all | solution.py:70
  212.6 12.3 %fusion.31 = f32[128,128,16,8]{1,0,3,2:T(8,128)} fusion(f32[128,16,128,8]{2,0,3,1:T(8,128)} %copy.82), kind=kOutput, calls=%fused_computation.48 | convolution fusion | flops 3221454848 | bytes 16777216 | tf_op jit(solution)/shard_map/pxyz,yk->pxkz/dot_general | solution.py:74
  224.9 88.9 %all-to-all-done = f32[128,16,8,128]{0,2,1,3:T(8,128)} async-done(((f32[128,16,8,128]{0,2,1,3:T(8,128)}), f32[128,16,8,128]{0,2,1,3:T(8,128)}, u32[]{:S(2)}, u32[]{:S(2)}) %all-to-all-start) | async-done | bytes 8388640 | tf_op jit(solution)/shard_map/all_to_all | solution.py:69
  313.8 11.5 %copy.75 = f32[128,16,16,8,8]{0,4,3,2,1:T(8,128)} copy(f32[128,16,16,8,8]{0,3,1,4,2:T(8,128)} %bitcast.6) | data formatting | bytes 16777216 | tf_op jit(solution)/shard_map/all_to_all | solution.py:69
  325.3 9.3 %copy.76 = f32[128,16,128,8]{2,0,3,1:T(8,128)} copy(f32[128,16,128,8]{0,3,2,1:T(8,128)} %bitcast.84) | data formatting | bytes 16777216 | tf_op jit(solution)/shard_map/all_to_all | solution.py:69
  334.5 12.4 %subtract_bitcast_fusion = f32[128,16,128,8]{0,2,3,1:T(8,128)S(1)} fusion(f32[128,128,16,8]{1,0,3,2:T(8,128)} %fusion.31, f32[128,16,128,8]{2,0,3,1:T(8,128)} %copy.76), kind=kOutput, calls=%fused_computation.7 | convolution fusion | flops 3223552000 | bytes 25165824 | tf_op jit(solution)/shard_map/pxyz,yk->pxkz/dot_general | solution.py:74
  347.0 8.1 %copy.89 = f32[128,16,128,8]{0,3,1,2:T(8,128)} copy(f32[128,16,128,8]{0,2,3,1:T(8,128)S(1)} %subtract_bitcast_fusion) | data formatting | bytes 16777216 | tf_op jit(solution)/shard_map/sub | solution.py:74
  360.6 10.0 %fusion.33 = f32[128,128,16,8]{1,0,3,2:T(8,128)S(1)} fusion(f32[128,16,128,8]{2,0,3,1:T(8,128)} %copy.76), kind=kOutput, calls=%fused_computation.50 | convolution fusion | flops 3221454848 | bytes 16777216 | tf_op jit(solution)/shard_map/pxyz,yk->pxkz/dot_general | solution.py:71
  370.6 10.3 %add_bitcast_fusion = f32[128,16,128,8]{0,2,3,1:T(8,128)S(1)} fusion(f32[128,128,16,8]{1,0,3,2:T(8,128)S(1)} %fusion.33, f32[128,16,128,8]{2,0,3,1:T(8,128)} %copy.82), kind=kOutput, calls=%fused_computation.8 | convolution fusion | flops 3223552000 | bytes 25165824 | tf_op jit(solution)/shard_map/pxyz,yk->pxkz/dot_general | solution.py:71
  380.9 8.1 %copy.83 = f32[128,16,128,8]{0,3,1,2:T(8,128)} copy(f32[128,16,128,8]{0,2,3,1:T(8,128)S(1)} %add_bitcast_fusion) | data formatting | bytes 16777216 | tf_op jit(solution)/shard_map/add | solution.py:71
  389.0 66.3 %all-to-all-done.3 = f32[128,16,128,8]{0,3,1,2:T(8,128)} async-done(((f32[128,16,128,8]{0,3,1,2:T(8,128)}), f32[128,16,128,8]{0,3,1,2:T(8,128)}, u32[]{:S(2)}, u32[]{:S(2)}) %all-to-all-start.3) | async-done | bytes 8388640 | tf_op jit(solution)/shard_map/all_to_all | solution.py:80
  462.1 7.8 %copy.91 = f32[128,8,16,16,8]{0,4,3,2,1:T(8,128)} copy(f32[128,8,16,16,8]{0,4,2,3,1:T(8,128)} %bitcast.26) | data formatting | bytes 16777216 | tf_op jit(solution)/shard_map/all_to_all | solution.py:80
  469.9 9.3 %copy.92 = f32[128,128,128]{1,0,2:T(8,128)} copy(f32[128,128,128]{0,2,1:T(8,128)} %bitcast.85) | data formatting | bytes 16777216 | tf_op jit(solution)/shard_map/reshape | solution.py:34
  479.2 75.7 %all-to-all-done.2 = f32[128,16,128,8]{0,3,1,2:T(8,128)} async-done(((f32[128,16,128,8]{0,3,1,2:T(8,128)}), f32[128,16,128,8]{0,3,1,2:T(8,128)}, u32[]{:S(2)}, u32[]{:S(2)}) %all-to-all-start.2) | async-done | bytes 8388640 | tf_op jit(solution)/shard_map/all_to_all | solution.py:79
  554.8 7.8 %copy.85 = f32[128,8,16,16,8]{0,4,3,2,1:T(8,128)} copy(f32[128,8,16,16,8]{0,4,2,3,1:T(8,128)} %bitcast.18) | data formatting | bytes 16777216 | tf_op jit(solution)/shard_map/all_to_all | solution.py:79
  562.6 9.3 %copy.86 = f32[128,128,128]{1,0,2:T(8,128)} copy(f32[128,128,128]{0,2,1:T(8,128)} %bitcast.86) | data formatting | bytes 16777216 | tf_op jit(solution)/shard_map/reshape | solution.py:33
  571.9 6.2 gather_fusion.3
  578.1 6.2 gather_fusion.2
  589.3 23.2 %all_gather.6 = f32[128,1024]{0,1:T(8,128)S(1)} all-gather(f32[128,64]{0,1:T(8,128)S(1)} %broadcast_multiply_fusion.1), channel_id=1, replica_groups=mesh['row'=8,'col'=16] {'col'}, dimensions={1}, use_global_device_ids=true | all-gather | bytes 557056 | tf_op jit(solution)/shard_map/all_gather | solution.py:89
  612.5 22.3 %all_gather.7 = f32[128,1024]{0,1:T(8,128)S(1)} all-gather(f32[128,64]{0,1:T(8,128)S(1)} %broadcast_multiply_fusion), channel_id=1, replica_groups=mesh['row'=8,'col'=16] {'col'}, dimensions={1}, use_global_device_ids=true | all-gather | bytes 557056 | tf_op jit(solution)/shard_map/all_gather | solution.py:90
  636.4 58.5 %all-reduce.3.cloned.1.call-done = (f32[128,512]{0,1:T(8,128)}, f32[128,512]{0,1:T(8,128)}) async-done(((f32[128,512]{0,1:T(8,128)}, f32[128,512]{0,1:T(8,128)}), (f32[128,512]{0,1:T(8,128)}, f32[128,512]{0,1:T(8,128)})) %all-reduce.3.cloned.1.call-update) | async-done | bytes 524304 | tf_op jit(solution)/shard_map/psum | solution.py:14
  (38 shorter events, 37.3 us)
Async XLA Ops:
  27.4 3.2 copy-start
  54.7 131.5 %all-to-all-start.1 = ((f32[128,16,8,128]{0,2,1,3:T(8,128)}), f32[128,16,8,128]{0,2,1,3:T(8,128)}, u32[]{:S(2)}, u32[]{:S(2)}) async-start(f32[128,16,8,128]{0,2,1,3:T(8,128)} %copy.79), calls=%async_computation.1 | async-start | bytes 16777216 | tf_op jit(solution)/shard_map/all_to_all | solution.py:70
  186.1 127.6 %all-to-all-start = ((f32[128,16,8,128]{0,2,1,3:T(8,128)}), f32[128,16,8,128]{0,2,1,3:T(8,128)}, u32[]{:S(2)}, u32[]{:S(2)}) async-start(f32[128,16,8,128]{0,2,1,3:T(8,128)} %copy.73), calls=%async_computation | async-start | bytes 16777216 | tf_op jit(solution)/shard_map/all_to_all | solution.py:69
  355.0 100.2 %all-to-all-start.3 = ((f32[128,16,128,8]{0,3,1,2:T(8,128)}), f32[128,16,128,8]{0,3,1,2:T(8,128)}, u32[]{:S(2)}, u32[]{:S(2)}) async-start(f32[128,16,128,8]{0,3,1,2:T(8,128)} %copy.89), calls=%async_computation.3 | async-start | bytes 16777216 | tf_op jit(solution)/shard_map/all_to_all | solution.py:80
  455.3 99.6 %all-to-all-start.2 = ((f32[128,16,128,8]{0,3,1,2:T(8,128)}), f32[128,16,128,8]{0,3,1,2:T(8,128)}, u32[]{:S(2)}, u32[]{:S(2)}) async-start(f32[128,16,128,8]{0,3,1,2:T(8,128)} %copy.83), calls=%async_computation.2 | async-start | bytes 16777216 | tf_op jit(solution)/shard_map/all_to_all | solution.py:79
  460.2 234.7 %all-reduce.3.cloned.1.call-start = ((), (), s32[]{:S(2)}) async-start(), calls=%async_computation.4 | async-start | bytes 1048576 | tf_op jit(solution)/shard_map/psum | solution.py:14
  584.3 51.9 %copy-start.3 = (s32[128]{0:T(128)S(1)}, s32[128]{0:T(128)}, u32[]{:S(2)}) copy-start(s32[128]{0:T(128)} %param.17) | copy-start | bytes 1540
  584.3 52.0 %copy-start.4 = (s32[128]{0:T(128)S(1)}, s32[128]{0:T(128)}, u32[]{:S(2)}) copy-start(s32[128]{0:T(128)} %param.16) | copy-start | bytes 1540
  584.3 52.0 %copy-start.5 = (f32[64]{0:T(128)S(1)}, f32[64]{0:T(128)}, u32[]{:S(2)}) copy-start(f32[64]{0:T(128)} %param.14) | copy-start | bytes 772
  584.3 52.0 %copy-start.6 = (f32[64]{0:T(128)S(1)}, f32[64]{0:T(128)}, u32[]{:S(2)}) copy-start(f32[64]{0:T(128)} %param.15) | copy-start | bytes 772
  694.9 9.4 %copy-start.1 = (f32[2,1024,512]{2,1,0:T(8,128)S(1)}, f32[2,1024,512]{2,1,0:T(8,128)}, u32[]{:S(2)}) copy-start(f32[2,1024,512]{2,1,0:T(8,128)} %param.19) | copy-start | bytes 12582916
  694.9 9.4 %copy-start.2 = (f32[128,512]{0,1:T(8,128)S(1)}, f32[128,512]{0,1:T(8,128)}, u32[]{:S(2)}) copy-start(f32[128,512]{0,1:T(8,128)} %get-tuple-element.10) | copy-start | bytes 786436
Sparse Core Ops, SparseCore 0:
  636.4 58.4 all-reduce.2
where the time goes:
time: 724 us; the launch traced here: 716 us
  waiting for transfers between devices  393 us (54%)
  local copies, waits for them, and re-layouts  139 us (19%)
  matrix products  82.4 us (11%)
  blocking collectives  45.5 us (6%)
  starting transfers between devices  23.7 us (3%)
  other arithmetic  18.6 us (3%)
  between operations  14.2 us (2%)
    all_to_all x1, waiting for transfers between devices, on_device(): lax.all_to_all(z_im, 'col', split_axis=3, concat_axis=2, tiled=True)  103 us
    all_to_all x1, waiting for transfers between devices, on_device(): lax.all_to_all(z_re, 'col', split_axis=3, concat_axis=2, tiled=True)  88.9 us
    all_to_all x1, waiting for transfers between devices, on_device(): lax.all_to_all(y_re, 'row', split_axis=2, concat_axis=1, tiled=True)  75.7 us
    all_to_all x1, waiting for transfers between devices, on_device(): lax.all_to_all(y_im, 'row', split_axis=2, concat_axis=1, tiled=True)  66.3 us
    psum x1, waiting for transfers between devices, spread(): return lax.psum(block, axis)  58.5 us
    all_gather x1, blocking collectives, on_device(): lax.all_gather(m_re, 'col', axis=1, tiled=True)  23.2 us
    all_gather x1, blocking collectives, on_device(): lax.all_gather(m_im, 'col', axis=1, tiled=True)  22.3 us
    all_to_all x2, local copies, waits for them, and re-layouts, on_device(): lax.all_to_all(z_re, 'col', split_axis=3, concat_axis=2, tiled=True)  20.7 us
  transfers between devices with their start and end apart: 5, of which 5 were waited for; matrix products, arithmetic and copies ran while one was open for 14% of the time, Pallas kernels for 0%

commit v1 on v0

--- a/solution.py
+++ b/solution.py
@@ -11,7 +11,7 @@
 
 def spread(block, axis, holder):
     block = jnp.where(lax.axis_index(axis) == holder, block, jnp.zeros_like(block))
-    return lax.psum(block, axis)
+    return jnp.sum(lax.all_gather(block, axis), axis=0)
 
 
 def dft_tables(length):

time: 724 us -> 696 us (0.961)
  waiting for transfers between devices: 393 us -> 358 us
    psum x1 -> x0, waiting for transfers between devices: 58.5 us -> none  [spread(): return lax.psum(block, axis)]
    all_gather x0 -> x2, waiting for transfers between devices: none -> 23.6 us  [spread(): return jnp.sum(lax.all_gather(block, axis), axis=0)]
  transfers between devices with their start and end apart: 5 -> 6, of which waited for: 5 -> 6; matrix products, arithmetic and copies ran while one was open for 14% -> 16% of each run, Pallas kernels for 0% -> 0%
where the time goes in v1:
time: 696 us; the launch traced here: 686 us
  waiting for transfers between devices  358 us (51%)
  local copies, waits for them, and re-layouts  144 us (21%)
  matrix products  82.2 us (12%)
  blocking collectives  45.4 us (7%)
  starting transfers between devices  23.7 us (3%)
  other arithmetic  19.6 us (3%)
  between operations  14.2 us (2%)
    all_to_all x1, waiting for transfers between devices, on_device(): lax.all_to_all(z_im, 'col', split_axis=3, concat_axis=2, tiled=True)  103 us
    all_to_all x1, waiting for transfers between devices, on_device(): lax.all_to_all(z_re, 'col', split_axis=3, concat_axis=2, tiled=True)  88.9 us
    all_to_all x1, waiting for transfers between devices, on_device(): lax.all_to_all(y_re, 'row', split_axis=2, concat_axis=1, tiled=True)  75.7 us
    all_to_all x1, waiting for transfers between devices, on_device(): lax.all_to_all(y_im, 'row', split_axis=2, concat_axis=1, tiled=True)  66.2 us
    all_gather x2, waiting for transfers between devices, spread(): return jnp.sum(lax.all_gather(block, axis), axis=0)  23.6 us
    all_gather x1, blocking collectives, on_device(): lax.all_gather(m_re, 'col', axis=1, tiled=True)  23.1 us
    all_gather x1, blocking collectives, on_device(): lax.all_gather(m_im, 'col', axis=1, tiled=True)  22.3 us
    all_to_all x2, local copies, waits for them, and re-layouts, on_device(): lax.all_to_all(z_re, 'col', split_axis=3, concat_axis=2, tiled=True)  20.8 us
  transfers between devices with their start and end apart: 6, of which 6 were waited for; matrix products, arithmetic and copies ran while one was open for 16% of the time, Pallas kernels for 0%

profile of v1, /device:TPU:0, one launch (start us, length us, event | category | flops | bytes accessed | tf_op | source)
XLA Modules:
  0.0 686.4 jit_solution(5161983749927553127)
XLA Ops:
  7.9 6.5 gather_fusion.1
  14.4 6.5 gather_fusion
  20.9 6.5 select_multiply_fusion
  30.7 14.8 %fusion.6 = f32[128,16,8,128]{3,0,2,1:T(8,128)} fusion(f32[128,16,8,128]{3,2,1,0:T(8,128)S(1)} %select_multiply_fusion), kind=kOutput, calls=%fused_computation.18 | convolution fusion | flops 3223552000 | bytes 16777216 | tf_op jit(solution)/shard_map/pxyz,zk->pxyk/dot_general | solution.py:68
  45.5 9.4 %copy.101 = f32[128,16,8,128]{0,2,1,3:T(8,128)} copy(f32[128,16,8,128]{3,0,2,1:T(8,128)} %fusion.6) | data formatting | bytes 16777216 | tf_op jit(solution)/shard_map/neg | solution.py:68
  54.9 7.4 %all-to-all-start.1 = ((f32[128,16,8,128]{0,2,1,3:T(8,128)}), f32[128,16,8,128]{0,2,1,3:T(8,128)}, u32[]{:S(2)}, u32[]{:S(2)}) async-start(f32[128,16,8,128]{0,2,1,3:T(8,128)} %copy.101), calls=%async_computation.1 | async-start | bytes 16777216 | tf_op jit(solution)/shard_map/all_to_all | solution.py:70
  62.3 11.3 %fusion.29 = f32[128,16,8,128]{3,2,1,0:T(8,128)} fusion(f32[128,16,8,128]{3,2,1,0:T(8,128)} %copy-done), kind=kOutput, calls=%fused_computation.48 | convolution fusion | flops 3221454848 | bytes 16777216 | tf_op jit(solution)/shard_map/pxyz,zk->pxyk/dot_general | solution.py:67
  73.6 9.4 %copy.95 = f32[128,16,8,128]{0,2,1,3:T(8,128)} copy(f32[128,16,8,128]{3,2,1,0:T(8,128)} %fusion.29) | data formatting | bytes 16777216 | tf_op jit(solution)/shard_map/pxyz,zk->pxyk/dot_general | solution.py:67
  83.0 103.4 %all-to-all-done.1 = f32[128,16,8,128]{0,2,1,3:T(8,128)} async-done(((f32[128,16,8,128]{0,2,1,3:T(8,128)}), f32[128,16,8,128]{0,2,1,3:T(8,128)}, u32[]{:S(2)}, u32[]{:S(2)}) %all-to-all-start.1) | async-done | bytes 8388640 | tf_op jit(solution)/shard_map/all_to_all | solution.py:70
  186.3 5.7 all-to-all-start
  192.1 11.5 %copy.103 = f32[128,16,16,8,8]{0,4,3,2,1:T(8,128)} copy(f32[128,16,16,8,8]{0,3,1,4,2:T(8,128)} %bitcast.13) | data formatting | bytes 16777216 | tf_op jit(solution)/shard_map/all_to_all | solution.py:70
  203.5 9.3 %copy.104 = f32[128,16,128,8]{2,0,3,1:T(8,128)} copy(f32[128,16,128,8]{0,3,2,1:T(8,128)} %bitcast.93) | data formatting | bytes 16777216 | tf_op jit(solution)/shard_map/all_to_all | solution.py:70
  212.8 12.3 %fusion.31 = f32[128,128,16,8]{1,0,3,2:T(8,128)} fusion(f32[128,16,128,8]{2,0,3,1:T(8,128)} %copy.104), kind=kOutput, calls=%fused_computation.50 | convolution fusion | flops 3221454848 | bytes 16777216 | tf_op jit(solution)/shard_map/pxyz,yk->pxkz/dot_general | solution.py:74
  225.1 88.9 %all-to-all-done = f32[128,16,8,128]{0,2,1,3:T(8,128)} async-done(((f32[128,16,8,128]{0,2,1,3:T(8,128)}), f32[128,16,8,128]{0,2,1,3:T(8,128)}, u32[]{:S(2)}, u32[]{:S(2)}) %all-to-all-start) | async-done | bytes 8388640 | tf_op jit(solution)/shard_map/all_to_all | solution.py:69
  314.0 11.5 %copy.97 = f32[128,16,16,8,8]{0,4,3,2,1:T(8,128)} copy(f32[128,16,16,8,8]{0,3,1,4,2:T(8,128)} %bitcast.6) | data formatting | bytes 16777216 | tf_op jit(solution)/shard_map/all_to_all | solution.py:69
  325.4 9.3 %copy.98 = f32[128,16,128,8]{2,0,3,1:T(8,128)} copy(f32[128,16,128,8]{0,3,2,1:T(8,128)} %bitcast.94) | data formatting | bytes 16777216 | tf_op jit(solution)/shard_map/all_to_all | solution.py:69
  334.7 12.4 %subtract_bitcast_fusion = f32[128,16,128,8]{0,2,3,1:T(8,128)S(1)} fusion(f32[128,128,16,8]{1,0,3,2:T(8,128)} %fusion.31, f32[128,16,128,8]{2,0,3,1:T(8,128)} %copy.98), kind=kOutput, calls=%fused_computation.7 | convolution fusion | flops 3223552000 | bytes 25165824 | tf_op jit(solution)/shard_map/pxyz,yk->pxkz/dot_general | solution.py:74
  347.2 8.1 %copy.111 = f32[128,16,128,8]{0,3,1,2:T(8,128)} copy(f32[128,16,128,8]{0,2,3,1:T(8,128)S(1)} %subtract_bitcast_fusion) | data formatting | bytes 16777216 | tf_op jit(solution)/shard_map/sub | solution.py:74
  360.8 10.0 %fusion.33 = f32[128,128,16,8]{1,0,3,2:T(8,128)S(1)} fusion(f32[128,16,128,8]{2,0,3,1:T(8,128)} %copy.98), kind=kOutput, calls=%fused_computation.52 | convolution fusion | flops 3221454848 | bytes 16777216 | tf_op jit(solution)/shard_map/pxyz,yk->pxkz/dot_general | solution.py:71
  370.8 10.3 %add_bitcast_fusion = f32[128,16,128,8]{0,2,3,1:T(8,128)S(1)} fusion(f32[128,128,16,8]{1,0,3,2:T(8,128)S(1)} %fusion.33, f32[128,16,128,8]{2,0,3,1:T(8,128)} %copy.104), kind=kOutput, calls=%fused_computation.8 | convolution fusion | flops 3223552000 | bytes 25165824 | tf_op jit(solution)/shard_map/pxyz,yk->pxkz/dot_general | solution.py:71
  381.2 8.1 %copy.105 = f32[128,16,128,8]{0,3,1,2:T(8,128)} copy(f32[128,16,128,8]{0,2,3,1:T(8,128)S(1)} %add_bitcast_fusion) | data formatting | bytes 16777216 | tf_op jit(solution)/shard_map/add | solution.py:71
  389.2 66.2 %all-to-all-done.3 = f32[128,16,128,8]{0,3,1,2:T(8,128)} async-done(((f32[128,16,128,8]{0,3,1,2:T(8,128)}), f32[128,16,128,8]{0,3,1,2:T(8,128)}, u32[]{:S(2)}, u32[]{:S(2)}) %all-to-all-start.3) | async-done | bytes 8388640 | tf_op jit(solution)/shard_map/all_to_all | solution.py:80
  462.3 7.8 %copy.113 = f32[128,8,16,16,8]{0,4,3,2,1:T(8,128)} copy(f32[128,8,16,16,8]{0,4,2,3,1:T(8,128)} %bitcast.26) | data formatting | bytes 16777216 | tf_op jit(solution)/shard_map/all_to_all | solution.py:80
  470.1 9.3 %copy.114 = f32[128,128,128]{1,0,2:T(8,128)} copy(f32[128,128,128]{0,2,1:T(8,128)} %bitcast.95) | data formatting | bytes 16777216 | tf_op jit(solution)/shard_map/reshape | solution.py:34
  479.4 75.7 %all-to-all-done.2 = f32[128,16,128,8]{0,3,1,2:T(8,128)} async-done(((f32[128,16,128,8]{0,3,1,2:T(8,128)}), f32[128,16,128,8]{0,3,1,2:T(8,128)}, u32[]{:S(2)}, u32[]{:S(2)}) %all-to-all-start.2) | async-done | bytes 8388640 | tf_op jit(solution)/shard_map/all_to_all | solution.py:79
  555.0 7.8 %copy.107 = f32[128,8,16,16,8]{0,4,3,2,1:T(8,128)} copy(f32[128,8,16,16,8]{0,4,2,3,1:T(8,128)} %bitcast.18) | data formatting | bytes 16777216 | tf_op jit(solution)/shard_map/all_to_all | solution.py:79
  562.8 9.3 %copy.108 = f32[128,128,128]{1,0,2:T(8,128)} copy(f32[128,128,128]{0,2,1:T(8,128)} %bitcast.96) | data formatting | bytes 16777216 | tf_op jit(solution)/shard_map/reshape | solution.py:33
  572.2 6.2 gather_fusion.3
  578.4 6.2 gather_fusion.2
  589.5 23.1 %all_gather.18 = f32[128,1024]{0,1:T(8,128)S(1)} all-gather(f32[128,64]{0,1:T(8,128)S(1)} %broadcast_multiply_fusion.1), channel_id=1, replica_groups=mesh['row'=8,'col'=16] {'col'}, dimensions={1}, use_global_device_ids=true | all-gather | bytes 557056 | tf_op jit(solution)/shard_map/all_gather | solution.py:89
  613.4 22.3 %all_gather.21 = f32[128,1024]{0,1:T(8,128)S(1)} all-gather(f32[128,64]{0,1:T(8,128)S(1)} %broadcast_multiply_fusion), channel_id=1, replica_groups=mesh['row'=8,'col'=16] {'col'}, dimensions={1}, use_global_device_ids=true | all-gather | bytes 557056 | tf_op jit(solution)/shard_map/all_gather | solution.py:90
  645.2 22.5 %all-gather.7.cloned.1.call-done = f32[1024,512]{0,1:T(8,128)} async-done(((f32[128,512]{0,1:T(8,128)}), f32[1024,512]{0,1:T(8,128)}) %all-gather.7.cloned.1.call-update) | async-done | bytes 2097168 | tf_op jit(solution)/shard_map/all_gather | solution.py:14
  (43 shorter events, 43.4 us)
Async XLA Ops:
  27.4 3.2 copy-start
  54.9 131.5 %all-to-all-start.1 = ((f32[128,16,8,128]{0,2,1,3:T(8,128)}), f32[128,16,8,128]{0,2,1,3:T(8,128)}, u32[]{:S(2)}, u32[]{:S(2)}) async-start(f32[128,16,8,128]{0,2,1,3:T(8,128)} %copy.101), calls=%async_computation.1 | async-start | bytes 16777216 | tf_op jit(solution)/shard_map/all_to_all | solution.py:70
  186.3 127.6 %all-to-all-start = ((f32[128,16,8,128]{0,2,1,3:T(8,128)}), f32[128,16,8,128]{0,2,1,3:T(8,128)}, u32[]{:S(2)}, u32[]{:S(2)}) async-start(f32[128,16,8,128]{0,2,1,3:T(8,128)} %copy.95), calls=%async_computation | async-start | bytes 16777216 | tf_op jit(solution)/shard_map/all_to_all | solution.py:69
  355.2 100.2 %all-to-all-start.3 = ((f32[128,16,128,8]{0,3,1,2:T(8,128)}), f32[128,16,128,8]{0,3,1,2:T(8,128)}, u32[]{:S(2)}, u32[]{:S(2)}) async-start(f32[128,16,128,8]{0,3,1,2:T(8,128)} %copy.111), calls=%async_computation.3 | async-start | bytes 16777216 | tf_op jit(solution)/shard_map/all_to_all | solution.py:80
  455.5 99.6 %all-to-all-start.2 = ((f32[128,16,128,8]{0,3,1,2:T(8,128)}), f32[128,16,128,8]{0,3,1,2:T(8,128)}, u32[]{:S(2)}, u32[]{:S(2)}) async-start(f32[128,16,128,8]{0,3,1,2:T(8,128)} %copy.105), calls=%async_computation.2 | async-start | bytes 16777216 | tf_op jit(solution)/shard_map/all_to_all | solution.py:79
  460.4 177.3 %all-gather.5.cloned.1.call-start = ((), (), s32[]{:S(2)}) async-start(), calls=%async_computation.4 | async-start | bytes 2359296 | tf_op jit(solution)/shard_map/all_gather | solution.py:14
  584.5 51.9 %copy-start.2 = (s32[128]{0:T(128)S(1)}, s32[128]{0:T(128)}, u32[]{:S(2)}) copy-start(s32[128]{0:T(128)} %param.17) | copy-start | bytes 1540
  584.5 51.9 %copy-start.3 = (s32[128]{0:T(128)S(1)}, s32[128]{0:T(128)}, u32[]{:S(2)}) copy-start(s32[128]{0:T(128)} %param.16) | copy-start | bytes 1540
  584.5 52.0 %copy-start.4 = (f32[64]{0:T(128)S(1)}, f32[64]{0:T(128)}, u32[]{:S(2)}) copy-start(f32[64]{0:T(128)} %param.14) | copy-start | bytes 772
  584.5 52.0 %copy-start.5 = (f32[64]{0:T(128)S(1)}, f32[64]{0:T(128)}, u32[]{:S(2)}) copy-start(f32[64]{0:T(128)} %param.15) | copy-start | bytes 772
  613.4 54.4 %all-gather.7.cloned.1.call-start = ((), (), s32[]{:S(2)}) async-start(), calls=%async_computation.5 | async-start | bytes 2359296 | tf_op jit(solution)/shard_map/all_gather | solution.py:14
  667.7 6.9 copy-start.1
Sparse Core Ops, SparseCore 0:
  613.5 24.1 all-gather.4
  639.4 28.2 all-gather.6
